TPU v7x, 512 devices: a whole 4x4x16 slice. The times are simulated.
512 devices in a mesh: grp: 4 (over y), seq: 32 (over z, core), mp: 4 (over x).
Axes of the slice: x: 4, y: 4, z: 16, core: 2. Of those that a mesh axis runs over, the one named last changes fastest.
Arguments:
- queries: bfloat16 [4, 4096, 2048], P('grp', 'seq', 'mp'), may hold values from -16 to 16
- d_out: bfloat16 [4, 4096, 2048], P('grp', 'seq', 'mp'), may hold values from -6 to 6
- neighbour_kv: bfloat16 [4, 256, 128, 2, 2048], P('grp', 'seq', None, None, 'mp'), may hold values from -16 to 16
- target: int32 [4, 256], P('grp', 'seq'), may hold values from -1 to 127, as said below
- bias: float32 [16, 191], P('mp'), may hold values from -6 to 6
Outputs:
- attended: bfloat16 [4, 4096, 2048], P('grp', 'seq', 'mp')
- d_query: bfloat16 [4, 4096, 2048], P('grp', 'seq', 'mp')
- d_kv: bfloat16 [4, 256, 128, 2, 2048], P('grp', 'seq', None, None, 'mp')
- d_bias: float32 [16, 191], P('mp')
Inputs may be any that keep to these rules, and one draw needn't show every extreme that they name: `target`: in each group every entry 0..127 stands in exactly one slot and -1 marks an empty slot. The slots of one index of seq hold at most 1 entries e with the same e // 4, and some index reaches that; some index of seq holds 8 entries.
All inputs are finite; a program needn't handle non-finite values.
Results may differ from a plain program's by a relative error of at most 0.011.
Values may be sent and summed in bfloat16 or wider, within the bound.
No kernel may reach another device: no remote copies, remote signals or barrier semaphores. Data moves between devices by JAX's collectives and lax.ppermute only.
A program may use at most 128 MiB of HBM per device.

v0:
```python
import jax
import jax.numpy as jnp
from jax import lax
from jax.sharding import PartitionSpec as P

STRETCH = 64
NB_LEN = 128


def passed_along(block, axis, distance):
    devices = range(lax.axis_size(axis))
    route = [(i - distance, i) for i in devices if i - distance in devices]
    return lax.ppermute(block, axis, route)


def bias_grid(lookup, row_count, col_count):
    head_num = lookup.shape[0]
    span = row_count + col_count
    padded = jnp.pad(lookup, ((0, 0), (0, 1)))
    flattened = jnp.tile(padded, (1, row_count))
    flattened = jnp.pad(flattened, ((0, 0), (0, row_count)))
    shaped = flattened.reshape(head_num, row_count, span + 1)[:, :, :col_count]
    return shaped[:, :, ::-1]


def bias_fold(grads):
    head_num, row_count, col_count = grads.shape
    turned = grads[:, :, ::-1]
    padded = jnp.pad(turned, ((0, 0), (0, 0), (0, row_count)))
    flattened = padded.reshape(head_num, row_count * (row_count + col_count))
    flattened = flattened[:, : row_count * (row_count + col_count - 1)]
    return jnp.sum(flattened.reshape(head_num, row_count, row_count + col_count - 1), axis=1)


def select_rows(picker, lookup):
    chosen = jnp.dot(
        picker.astype(lookup.dtype),
        lookup,
        preferred_element_type=jnp.float32,
        precision=lax.Precision.HIGHEST,
    )
    return chosen.astype(lookup.dtype)


def slot_places(target_row, owners, capacity, per_owner):
    is_used = target_row >= 0
    owner_of = jnp.where(is_used, target_row // per_owner, -1)
    positions = jnp.arange(target_row.shape[0])
    earlier = (
        (positions[None, :] < positions[:, None])
        & (owner_of[None, :] == owner_of[:, None])
        & is_used[None, :]
    )
    rank_of = jnp.sum(earlier.astype(jnp.int32), axis=1)
    match_owner = owner_of[None, :] == jnp.arange(owners)[:, None]
    match_rank = rank_of[None, :] == jnp.arange(capacity)[:, None]
    return match_owner[:, None, :] & match_rank[None, :, :] & is_used[None, None, :]


def local(queries, d_out, neighbour_kv, target, bias):
    tok_rows = queries.shape[1]
    width_dev = queries.shape[2]
    head_count = bias.shape[0]
    head_depth = width_dev // head_count
    stretch_count = tok_rows // STRETCH
    per_owner = 2 * stretch_count
    shard_count = lax.axis_size("seq")
    my_index = lax.axis_index("seq")
    group_size = min(shard_count, per_owner)
    capacity = (per_owner + group_size - 1) // group_size
    seq_stretches = min(2048, tok_rows * shard_count) // STRETCH
    scale_factor = head_depth ** (-0.5)
    bias_rows = bias_grid(bias, STRETCH, NB_LEN).transpose(1, 0, 2)
    q_rows = queries[0]
    g_rows = d_out[0]
    next_pair = passed_along(jnp.stack([q_rows[:STRETCH], g_rows[:STRETCH]]), "seq", -1)
    row_ids = jnp.arange(STRETCH)
    stretch_ids = my_index * stretch_count + jnp.arange(stretch_count)
    is_live = (row_ids[None, :] == 0) | ((stretch_ids[:, None] + 1) % seq_stretches != 0)
    live_rows = is_live.astype(jnp.float32)
    q_win = jnp.concatenate([q_rows, next_pair[0]])[STRETCH - 1 : STRETCH - 1 + tok_rows]
    q_win = q_win.reshape(stretch_count, STRETCH * width_dev)
    g_win = jnp.concatenate([g_rows, next_pair[1]])[STRETCH - 1 : STRETCH - 1 + tok_rows]
    g_win = g_win.reshape(stretch_count, STRETCH, width_dev) * is_live[:, :, None].astype(
        jnp.bfloat16
    )
    g_win = g_win.reshape(stretch_count, STRETCH * width_dev)
    my_targets = target[0]
    slot_count = my_targets.shape[0]
    send_map = slot_places(my_targets, shard_count, capacity, per_owner)
    id_buffer = jnp.sum(jnp.where(send_map, my_targets[None, None, :] + 1, 0), axis=2) - 1
    recv_ids = lax.all_to_all(id_buffer, "seq", split_axis=0, concat_axis=0, tiled=True)
    flat_ids = recv_ids.reshape(shard_count * capacity)
    has_entry = flat_ids >= 0
    local_entry = flat_ids - my_index * per_owner
    entry_pick = (local_entry[:, None] == jnp.arange(per_owner)[None, :]) & has_entry[:, None]
    stretch_pick = (local_entry[:, None] // 2 == jnp.arange(stretch_count)[None, :]) & has_entry[
        :, None
    ]
    back_pick = send_map.reshape(shard_count * capacity, slot_count)
    slot_pick = back_pick.T
    q_send = select_rows(stretch_pick, q_win).reshape(shard_count, capacity, STRETCH * width_dev)
    g_send = select_rows(stretch_pick, g_win).reshape(shard_count, capacity, STRETCH * width_dev)
    q_recv, g_recv = (
        lax.all_to_all(q_send, "seq", split_axis=0, concat_axis=0, tiled=True),
        lax.all_to_all(g_send, "seq", split_axis=0, concat_axis=0, tiled=True),
    )
    q_slots = select_rows(slot_pick, q_recv.reshape(shard_count * capacity, -1))
    q_slots = q_slots.reshape(slot_count, STRETCH, head_count, head_depth)
    stored = neighbour_kv[0]
    key_rows = stored[:, :, 0].reshape(slot_count, NB_LEN, head_count, head_depth)
    value_rows = stored[:, :, 1].reshape(slot_count, NB_LEN, head_count, head_depth)
    scores = jnp.einsum("sihd,sjhd->sihj", q_slots, key_rows, preferred_element_type=jnp.float32)
    scores = scores * scale_factor + bias_rows[None]
    peak_val = jnp.max(scores, axis=-1)
    weights = jnp.exp(scores - peak_val[..., None])
    row_total = jnp.sum(weights, axis=-1)
    partial_value = jnp.einsum(
        "sihj,sjhd->sihd",
        weights.astype(jnp.bfloat16),
        value_rows,
        preferred_element_type=jnp.float32,
    )
    part_send = select_rows(back_pick, partial_value.reshape(slot_count, -1)).reshape(
        shard_count, capacity, -1
    )
    peak_send = select_rows(back_pick, peak_val.reshape(slot_count, -1)).reshape(
        shard_count, capacity, -1
    )
    total_send = select_rows(back_pick, row_total.reshape(slot_count, -1)).reshape(
        shard_count, capacity, -1
    )
    part_recv, peak_recv, total_recv = (
        lax.all_to_all(part_send, "seq", split_axis=0, concat_axis=0, tiled=True),
        lax.all_to_all(peak_send, "seq", split_axis=0, concat_axis=0, tiled=True),
        lax.all_to_all(total_send, "seq", split_axis=0, concat_axis=0, tiled=True),
    )
    entry_back = entry_pick.T
    parts_own = select_rows(entry_back, part_recv.reshape(shard_count * capacity, -1))
    parts_own = parts_own.reshape(stretch_count, 2, STRETCH, head_count, head_depth)
    peaks_own = select_rows(entry_back, peak_recv.reshape(shard_count * capacity, -1))
    peaks_own = peaks_own.reshape(stretch_count, 2, STRETCH, head_count)
    totals_own = select_rows(entry_back, total_recv.reshape(shard_count * capacity, -1))
    totals_own = totals_own.reshape(stretch_count, 2, STRETCH, head_count)
    top_peak = jnp.max(peaks_own, axis=1)
    factor = jnp.exp(peaks_own - top_peak[:, None])
    denominator = jnp.sum(factor * totals_own, axis=1)
    combined = jnp.sum(factor[..., None] * parts_own, axis=1) / denominator[..., None]
    combined = combined * live_rows[:, :, None, None]
    att_win = combined.astype(jnp.bfloat16).reshape(tok_rows, width_dev)
    att_before = passed_along(att_win[tok_rows - STRETCH :], "seq", 1)
    log_total = top_peak + jnp.log(denominator)
    g_wide = g_win.reshape(stretch_count, STRETCH, head_count, head_depth).astype(jnp.float32)
    inner_dot = jnp.sum(g_wide * combined, axis=-1)
    row_stats = jnp.repeat(jnp.stack([log_total, inner_dot], axis=1), 2, axis=0)
    stats_send = select_rows(entry_pick, row_stats.reshape(per_owner, -1)).reshape(
        shard_count, capacity, -1
    )
    stats_recv = lax.all_to_all(stats_send, "seq", split_axis=0, concat_axis=0, tiled=True)
    g_slots = select_rows(slot_pick, g_recv.reshape(shard_count * capacity, -1))
    g_slots = g_slots.reshape(slot_count, STRETCH, head_count, head_depth)
    stats_slots = select_rows(slot_pick, stats_recv.reshape(shard_count * capacity, -1))
    stats_slots = stats_slots.reshape(slot_count, 2, STRETCH, head_count)
    prob_full = jnp.exp(scores - stats_slots[:, 0][..., None])
    prob_low = prob_full.astype(jnp.bfloat16)
    grad_values = jnp.einsum(
        "sihj,sihd->sjhd", prob_low, g_slots, preferred_element_type=jnp.float32
    )
    grad_prob = jnp.einsum(
        "sihd,sjhd->sihj", g_slots, value_rows, preferred_element_type=jnp.float32
    )
    grad_scores = prob_full * (grad_prob - stats_slots[:, 1][..., None])
    scores_low = grad_scores.astype(jnp.bfloat16)
    grad_rows = (
        jnp.einsum("sihj,sjhd->sihd", scores_low, key_rows, preferred_element_type=jnp.float32)
        * scale_factor
    )
    grad_keys = (
        jnp.einsum("sihj,sihd->sjhd", scores_low, q_slots, preferred_element_type=jnp.float32)
        * scale_factor
    )
    d_kv = jnp.stack(
        [
            grad_keys.reshape(slot_count, NB_LEN, width_dev),
            grad_values.reshape(slot_count, NB_LEN, width_dev),
        ],
        axis=2,
    ).astype(jnp.bfloat16)
    bias_part = bias_fold(jnp.sum(grad_scores, axis=0).transpose(1, 0, 2))
    rows_send = select_rows(back_pick, grad_rows.reshape(slot_count, -1)).reshape(
        shard_count, capacity, -1
    )
    rows_recv = lax.all_to_all(rows_send, "seq", split_axis=0, concat_axis=0, tiled=True)
    grad_entries = select_rows(entry_back, rows_recv.reshape(shard_count * capacity, -1))
    grad_entries = grad_entries.reshape(stretch_count, 2, STRETCH * width_dev)
    grad_win = (
        (grad_entries[:, 0] + grad_entries[:, 1]).astype(jnp.bfloat16).reshape(tok_rows, width_dev)
    )
    grad_before = passed_along(grad_win[tok_rows - STRETCH :], "seq", 1)
    attended = jnp.concatenate([att_before[1:], att_win[: tok_rows - STRETCH + 1]])
    d_query = jnp.concatenate([grad_before[1:], grad_win[: tok_rows - STRETCH + 1]])
    raw_sum = lax.psum(bias_part, ("grp", "seq"))
    squares = lax.psum(jnp.sum(raw_sum * raw_sum), "mp")
    d_bias = raw_sum * jnp.minimum(1.0, 1.0 / jnp.sqrt(squares + 1e-12))
    return (attended[None], d_query[None], d_kv[None], d_bias)


def solution(mesh):
    in_specs = (
        P("grp", "seq", "mp"),
        P("grp", "seq", "mp"),
        P("grp", "seq", None, None, "mp"),
        P("grp", "seq"),
        P("mp", None),
    )
    out_specs = (
        P("grp", "seq", "mp"),
        P("grp", "seq", "mp"),
        P("grp", "seq", None, None, "mp"),
        P("mp", None),
    )
    return jax.shard_map(local, mesh=mesh, in_specs=in_specs, out_specs=out_specs, check_vma=False)
```

profile of v0, /device:TPU:1, one launch (start us, length us, event | category | flops | bytes accessed | tf_op | source)
XLA Modules:
  0.0 1025.3 jit_solution(9001594490378168722)
XLA Ops:
  3.6 0.7 copy.156
  4.3 16.7 %all-to-all-start = ((s32[32,1,1]{2,1,0:T(1,128)}), s32[32,1,1]{2,1,0:T(1,128)S(1)}, u32[]{:S(2)}, u32[]{:S(2)}) async-start(s32[32,1,1]{2,1,0:T(1,128)} %copy.156), calls=%async_computation | async-start | bytes 32768 | tf_op jit(solution)/shard_map/all_to_all | solution.py:92
  21.0 0.8 slice.70
  21.9 0.8 slice.69
  22.7 2.1 collective-permute-start
  24.9 7.8 all-to-all-done
  34.1 0.9 pad_maximum_fusion.2
  35.1 0.7 fusion
  36.4 2.9 reduce.9
  39.3 4.5 reshape.685
  43.8 6.9 all-to-all-start.1
  51.2 2.1 fusion.1
  53.3 4.5 reduce.10
  57.8 4.5 reshape.687
  62.3 87.0 %all-to-all-done.1 = bf16[32,2,16384]{2,1,0:T(2,128)(2,1)S(1)} async-done(((bf16[32,2,16384]{2,1,0:T(2,128)(2,1)}), bf16[32,2,16384]{2,1,0:T(2,128)(2,1)S(1)}, u32[]{:S(2)}, u32[]{:S(2)}) %all-to-all-start.1) | async-done | bytes 2097184 | tf_op jit(solution)/shard_map/all_to_all | solution.py:105
  149.3 5.2 all-to-all-start.6
  154.5 6.2 copy.158
  161.5 2.7 fusion.78
  164.1 10.5 %reshape.686 = bf16[32,1,32768]{2,1,0:T(2,128)(2,1)} reshape(bf16[32,2,16384]{2,1,0:T(2,128)(2,1)} %copy-done) | data formatting | bytes 4194304
  174.6 4.5 convolution_convert_fusion.3
  179.1 0.8 copy-done.4
  179.9 1.9 fusion.79
  182.7 1.8 convolution_bitcast_fusion.3
  184.6 69.2 %all-to-all-done.6 = bf16[32,2,16384]{2,1,0:T(2,128)(2,1)} async-done(((bf16[32,2,16384]{2,1,0:T(2,128)(2,1)}), bf16[32,2,16384]{2,1,0:T(2,128)(2,1)}, u32[]{:S(2)}, u32[]{:S(2)}) %all-to-all-start.6) | async-done | bytes 2097184 | tf_op jit(solution)/shard_map/all_to_all | solution.py:106
  253.8 6.3 all-to-all-start.2
  260.7 2.9 copy.167
  263.6 2.7 reshape.655
  267.3 5.0 all-to-all-done.2
  272.3 7.3 all-to-all-start.4
  279.6 3.1 convolution_bitcast_fusion.1
  282.7 6.3 copy.168
  289.0 2.7 all-to-all-done.4
  291.7 9.9 all-to-all-start.3
  301.7 10.5 %reshape.688 = bf16[32,1,32768]{2,1,0:T(2,128)(2,1)} reshape(bf16[32,2,16384]{2,1,0:T(2,128)(2,1)} %all-to-all-done.6) | data formatting | bytes 4194304
  313.4 171.4 %all-to-all-done.3 = f32[32,1,32768]{2,1,0:T(1,128)} async-done(((f32[32,1,32768]{2,1,0:T(1,128)}), f32[32,1,32768]{2,1,0:T(1,128)}, u32[]{:S(2)}, u32[]{:S(2)}) %all-to-all-start.3) | async-done | bytes 4194336 | tf_op jit(solution)/shard_map/all_to_all | solution.py:134
  484.7 6.6 copy.249
  491.3 6.0 dot_general.86
  497.4 6.8 fusion.20
  504.1 1.1 multiply_reduce_fusion
  505.9 0.7 copy.177
  506.6 10.9 %all-to-all-start.5 = ((f32[32,1,512]{2,1,0:T(1,128)}), f32[32,1,512]{2,1,0:T(1,128)S(1)}, u32[]{:S(2)}, u32[]{:S(2)}) async-start(f32[32,1,512]{2,1,0:T(1,128)} %copy.177), calls=%async_computation.5 | async-start | bytes 131072 | tf_op jit(solution)/shard_map/all_to_all | solution.py:159
  517.5 4.5 convolution_convert_fusion.2
  522.0 8.5 all-to-all-done.5
  531.1 0.8 fusion.81
  531.9 0.8 copy-done.3
  532.7 2.0 fusion.12
  534.8 0.7 copy.186
  535.5 1.5 reshape.668
  537.0 3.1 convolution_bitcast_fusion
  540.1 6.3 copy.187
  546.4 6.1 all-to-all-start.7
  552.9 3.7 collective-permute-start.1
  556.7 169.2 %collective-permute-done.1 = bf16[64,512]{1,0:T(8,128)(2,1)S(1)} collective-permute-done((bf16[64,512]{1,0:T(8,128)(2,1)S(1)}, bf16[64,512]{1,0:T(8,128)(2,1)S(1)}, u32[]{:S(2)}, u32[]{:S(2)}) %collective-permute-start.1) | collective-permute-done | bytes 65568 | tf_op jit(solution)/shard_map/ppermute | solution.py:13
  726.5 256.5 %psum.14 = f32[4,191]{1,0:T(4,128)S(1)} all-reduce(f32[4,191]{1,0:T(4,128)S(1)} %reduce_sum.88), channel_id=1, replica_groups=mesh['grp'=4,'seq'=32,'mp'=4] {'grp','seq'}, use_global_device_ids=true, to_apply=%region_10.11 | all-reduce | flops 764 | bytes 6112 | tf_op jit(solution)/shard_map/psum | solution.py:202
  984.3 9.1 psum.15
  993.4 1.8 convolution_convert_fusion.4
  995.2 4.6 copy.191
  999.8 1.8 multiply_convert_fusion
  1001.6 3.8 copy.190
  1006.1 6.7 pad_maximum_fusion
  1012.8 6.0 fusion.2
  1018.8 1.0 fusion.76
  1020.3 1.9 collective-permute-start.2
  1022.9 1.6 collective-permute-done.2
  (99 shorter events, 15.2 us)
Async XLA Ops:
  4.3 28.5 %all-to-all-start = ((s32[32,1,1]{2,1,0:T(1,128)}), s32[32,1,1]{2,1,0:T(1,128)S(1)}, u32[]{:S(2)}, u32[]{:S(2)}) async-start(s32[32,1,1]{2,1,0:T(1,128)} %copy.156), calls=%async_computation | async-start | bytes 32768 | tf_op jit(solution)/shard_map/all_to_all | solution.py:92
  22.7 11.4 %collective-permute-start = (bf16[2,64,512]{2,1,0:T(8,128)(2,1)S(1)}, bf16[2,64,512]{2,1,0:T(8,128)(2,1)S(1)}, u32[]{:S(2)}, u32[]{:S(2)}) collective-permute-start(bf16[2,64,512]{2,1,0:T(8,128)(2,1)S(1)} %pad_maximum_fusion.3), channel_id=1, source_target_pairs={{4,0},{8,4},{12,8},{16,12},{20,16},{24,20},{28,24},{32,28},{36,32}... | collective-permute-start | bytes 393224 | tf_op jit(solution)/shard_map/ppermute | solution.py:13
  39.3 11.7 %copy-start.5 = (bf16[1,128,512]{2,1,0:T(8,128)(2,1)S(1)}, bf16[1,128,512]{2,1,0:T(8,128)(2,1)}, u32[]{:S(2)}) copy-start(bf16[1,128,512]{2,1,0:T(8,128)(2,1)} %param.6) | copy-start | bytes 393220
  43.8 105.5 %all-to-all-start.1 = ((bf16[32,2,16384]{2,1,0:T(2,128)(2,1)}), bf16[32,2,16384]{2,1,0:T(2,128)(2,1)S(1)}, u32[]{:S(2)}, u32[]{:S(2)}) async-start(bf16[32,2,16384]{2,1,0:T(2,128)(2,1)} %reshape.685), calls=%async_computation.1 | async-start | bytes 4194304 | tf_op jit(solution)/shard_map/all_to_all | solution.py:105
  62.3 98.4 %copy-start.7 = (f32[4,191]{1,0:T(4,128)S(1)}, f32[4,191]{1,0:T(4,128)}, u32[]{:S(2)}) copy-start(f32[4,191]{1,0:T(4,128)} %param.9) | copy-start | bytes 9172
  149.3 11.4 %copy-start = (bf16[32,2,16384]{2,1,0:T(2,128)(2,1)}, bf16[32,2,16384]{2,1,0:T(2,128)(2,1)S(1)}, u32[]{:S(2)}) copy-start(bf16[32,2,16384]{2,1,0:T(2,128)(2,1)S(1)} %all-to-all-done.1) | copy-start | bytes 6291460
  149.3 104.5 %all-to-all-start.6 = ((bf16[32,2,16384]{2,1,0:T(2,128)(2,1)}), bf16[32,2,16384]{2,1,0:T(2,128)(2,1)}, u32[]{:S(2)}, u32[]{:S(2)}) async-start(bf16[32,2,16384]{2,1,0:T(2,128)(2,1)} %reshape.687), calls=%async_computation.6 | async-start | bytes 4194304 | tf_op jit(solution)/shard_map/all_to_all | solution.py:106
  179.1 0.8 copy-start.4
  253.8 18.5 %all-to-all-start.2 = ((f32[32,1,256]{2,1,0:T(1,128)}), f32[32,1,256]{2,1,0:T(1,128)S(1)}, u32[]{:S(2)}, u32[]{:S(2)}) async-start(f32[32,1,256]{2,1,0:T(1,128)} %copy.162), calls=%async_computation.2 | async-start | bytes 65536 | tf_op jit(solution)/shard_map/all_to_all | solution.py:135
  272.3 19.4 %all-to-all-start.4 = ((f32[32,1,256]{2,1,0:T(1,128)}), f32[32,1,256]{2,1,0:T(1,128)S(1)}, u32[]{:S(2)}, u32[]{:S(2)}) async-start(f32[32,1,256]{2,1,0:T(1,128)} %copy.171), calls=%async_computation.4 | async-start | bytes 65536 | tf_op jit(solution)/shard_map/all_to_all | solution.py:136
  291.7 193.0 %all-to-all-start.3 = ((f32[32,1,32768]{2,1,0:T(1,128)}), f32[32,1,32768]{2,1,0:T(1,128)}, u32[]{:S(2)}, u32[]{:S(2)}) async-start(f32[32,1,32768]{2,1,0:T(1,128)} %copy.168), calls=%async_computation.3 | async-start | bytes 8388608 | tf_op jit(solution)/shard_map/all_to_all | solution.py:134
  506.6 23.9 %all-to-all-start.5 = ((f32[32,1,512]{2,1,0:T(1,128)}), f32[32,1,512]{2,1,0:T(1,128)S(1)}, u32[]{:S(2)}, u32[]{:S(2)}) async-start(f32[32,1,512]{2,1,0:T(1,128)} %copy.177), calls=%async_computation.5 | async-start | bytes 131072 | tf_op jit(solution)/shard_map/all_to_all | solution.py:159
  522.0 13.5 %copy-start.1 = (bf16[8,32768]{1,0:T(8,128)(2,1)}, bf16[8,32768]{1,0:T(8,128)(2,1)S(1)}, u32[]{:S(2)}) copy-start(bf16[8,32768]{1,0:T(8,128)(2,1)S(1)} %convolution_convert_fusion.2) | copy-start | bytes 1572868
  531.9 0.8 copy-start.3
  546.4 6.4 copy-start.6
  546.4 447.1 %copy-start.2 = (bf16[8,32768]{1,0:T(8,128)(2,1)S(1)}, bf16[8,32768]{1,0:T(8,128)(2,1)}, u32[]{:S(2)}) copy-start(bf16[8,32768]{1,0:T(8,128)(2,1)} %copy-done.1) | copy-start | bytes 1572868
  546.4 466.4 %all-to-all-start.7 = ((f32[32,1,32768]{2,1,0:T(1,128)}), f32[32,1,32768]{2,1,0:T(1,128)}, u32[]{:S(2)}, u32[]{:S(2)}) async-start(f32[32,1,32768]{2,1,0:T(1,128)} %copy.187), calls=%async_computation.7 | async-start | bytes 8388608 | tf_op jit(solution)/shard_map/all_to_all | solution.py:193
  552.9 173.0 %collective-permute-start.1 = (bf16[64,512]{1,0:T(8,128)(2,1)S(1)}, bf16[64,512]{1,0:T(8,128)(2,1)S(1)}, u32[]{:S(2)}, u32[]{:S(2)}) collective-permute-start(bf16[64,512]{1,0:T(8,128)(2,1)S(1)} %bitcast.224), channel_id=1, source_target_pairs={{0,4},{4,8},{8,12},{12,16},{16,20},{20,24},{24,28},{28,32},{32,36}... | collective-permute-start | bytes 196616 | tf_op jit(solution)/shard_map/ppermute | solution.py:13
  1020.3 4.2 collective-permute-start.2
where the time goes:
time: 1040 us; the launch traced here: 1030 us
  waiting for transfers between devices  522 us (50%)
  blocking collectives  266 us (26%)
  local copies, waits for them, and re-layouts  90.5 us (9%)
  starting transfers between devices  77.1 us (7%)
  matrix products  42.5 us (4%)
  other arithmetic  25.1 us (2%)
    psum x1, blocking collectives, local(): raw_sum = lax.psum(bias_part, ('grp', 'seq'))  257 us
    all_to_all x1, waiting for transfers between devices, local(): lax.all_to_all(part_send, 'seq', split_axis=0, concat_axis=0, tiled=True)  171 us
    ppermute x3, waiting for transfers between devices, passed_along(): return lax.ppermute(block, axis, route)  171 us
    all_to_all x1, waiting for transfers between devices, local(): lax.all_to_all(q_send, 'seq', split_axis=0, concat_axis=0, tiled=True)  87 us
    all_to_all x1, waiting for transfers between devices, local(): lax.all_to_all(g_send, 'seq', split_axis=0, concat_axis=0, tiled=True)  69.2 us
    unnamed x26, local copies, waits for them, and re-layouts  44.6 us
    dot_general x14, matrix products, select_rows(): jnp.dot(picker.astype(lookup.dtype), lookup, preferred_element_type=jnp.f...  32.4 us
  transfers between devices with their start and end apart: 11, of which 9 were waited for; matrix products, arithmetic and copies ran while one was open for 10% of the time, Pallas kernels for 0%

commit v1 on v0

--- a/solution.py
+++ b/solution.py
@@ -199,7 +199,8 @@
     grad_before = passed_along(grad_win[tok_rows - STRETCH :], "seq", 1)
     attended = jnp.concatenate([att_before[1:], att_win[: tok_rows - STRETCH + 1]])
     d_query = jnp.concatenate([grad_before[1:], grad_win[: tok_rows - STRETCH + 1]])
-    raw_sum = lax.psum(bias_part, ("grp", "seq"))
+    half = lax.psum(bias_part, "grp")
+    raw_sum = lax.psum(half, "seq")
     squares = lax.psum(jnp.sum(raw_sum * raw_sum), "mp")
     d_bias = raw_sum * jnp.minimum(1.0, 1.0 / jnp.sqrt(squares + 1e-12))
     return (attended[None], d_query[None], d_kv[None], d_bias)

time: 1040 us -> 846 us (0.81)
  blocking collectives: 266 us -> 75 us
    psum x1 -> x2, blocking collectives: 257 us -> 65.9 us  [the longest x1 56.8 us: local(): raw_sum = lax.psum(half, 'seq')]
  transfers between devices with their start and end apart: 11 -> 11, of which waited for: 9 -> 9; matrix products, arithmetic and copies ran while one was open for 10% -> 12% of each run, Pallas kernels for 0% -> 0%
where the time goes in v1:
time: 846 us; the launch traced here: 835 us
  waiting for transfers between devices  522 us (62%)
  local copies, waits for them, and re-layouts  90.5 us (11%)
  starting transfers between devices  77.4 us (9%)
  blocking collectives  75 us (9%)
  matrix products  42.5 us (5%)
  other arithmetic  25.1 us (3%)
    all_to_all x1, waiting for transfers between devices, local(): lax.all_to_all(part_send, 'seq', split_axis=0, concat_axis=0, tiled=True)  171 us
    ppermute x3, waiting for transfers between devices, passed_along(): return lax.ppermute(block, axis, route)  170 us
    all_to_all x1, waiting for transfers between devices, local(): lax.all_to_all(q_send, 'seq', split_axis=0, concat_axis=0, tiled=True)  87 us
    all_to_all x1, waiting for transfers between devices, local(): lax.all_to_all(g_send, 'seq', split_axis=0, concat_axis=0, tiled=True)  69.2 us
    psum x1, blocking collectives, local(): raw_sum = lax.psum(half, 'seq')  56.8 us
    unnamed x26, local copies, waits for them, and re-layouts  44.6 us
    dot_general x14, matrix products, select_rows(): jnp.dot(picker.astype(lookup.dtype), lookup, preferred_element_type=jnp.f...  32.4 us
  transfers between devices with their start and end apart: 11, of which 9 were waited for; matrix products, arithmetic and copies ran while one was open for 12% of the time, Pallas kernels for 0%

profile of v1, /device:TPU:1, one launch (start us, length us, event | category | flops | bytes accessed | tf_op | source)
XLA Modules:
  0.0 834.7 jit_solution(17391214607842558193)
XLA Ops:
  3.6 0.7 copy.156
  4.3 16.7 %all-to-all-start = ((s32[32,1,1]{2,1,0:T(1,128)}), s32[32,1,1]{2,1,0:T(1,128)S(1)}, u32[]{:S(2)}, u32[]{:S(2)}) async-start(s32[32,1,1]{2,1,0:T(1,128)} %copy.156), calls=%async_computation | async-start | bytes 32768 | tf_op jit(solution)/shard_map/all_to_all | solution.py:92
  21.0 0.8 slice.70
  21.9 0.8 slice.69
  22.7 2.1 collective-permute-start
  24.9 7.8 all-to-all-done
  34.1 0.9 pad_maximum_fusion.2
  35.1 0.7 fusion
  36.4 2.9 reduce.9
  39.3 4.5 reshape.685
  43.8 6.9 all-to-all-start.1
  51.2 2.1 fusion.1
  53.3 4.5 reduce.10
  57.8 4.5 reshape.687
  62.3 87.0 %all-to-all-done.1 = bf16[32,2,16384]{2,1,0:T(2,128)(2,1)S(1)} async-done(((bf16[32,2,16384]{2,1,0:T(2,128)(2,1)}), bf16[32,2,16384]{2,1,0:T(2,128)(2,1)S(1)}, u32[]{:S(2)}, u32[]{:S(2)}) %all-to-all-start.1) | async-done | bytes 2097184 | tf_op jit(solution)/shard_map/all_to_all | solution.py:105
  149.3 5.2 all-to-all-start.6
  154.5 6.2 copy.158
  161.5 2.7 fusion.78
  164.1 10.5 %reshape.686 = bf16[32,1,32768]{2,1,0:T(2,128)(2,1)} reshape(bf16[32,2,16384]{2,1,0:T(2,128)(2,1)} %copy-done) | data formatting | bytes 4194304
  174.6 4.5 convolution_convert_fusion.3
  179.1 0.8 copy-done.4
  179.9 1.9 fusion.79
  182.7 1.8 convolution_bitcast_fusion.3
  184.6 69.2 %all-to-all-done.6 = bf16[32,2,16384]{2,1,0:T(2,128)(2,1)} async-done(((bf16[32,2,16384]{2,1,0:T(2,128)(2,1)}), bf16[32,2,16384]{2,1,0:T(2,128)(2,1)}, u32[]{:S(2)}, u32[]{:S(2)}) %all-to-all-start.6) | async-done | bytes 2097184 | tf_op jit(solution)/shard_map/all_to_all | solution.py:106
  253.8 6.3 all-to-all-start.2
  260.7 2.9 copy.167
  263.6 2.7 reshape.655
  267.3 5.0 all-to-all-done.2
  272.3 7.3 all-to-all-start.4
  279.6 3.1 convolution_bitcast_fusion.1
  282.7 6.3 copy.168
  289.0 2.7 all-to-all-done.4
  291.7 9.9 %all-to-all-start.3 = ((f32[32,1,32768]{2,1,0:T(1,128)}), f32[32,1,32768]{2,1,0:T(1,128)}, u32[]{:S(2)}, u32[]{:S(2)}) async-start(f32[32,1,32768]{2,1,0:T(1,128)} %copy.168), calls=%async_computation.3 | async-start | bytes 8388608 | tf_op jit(solution)/shard_map/all_to_all | solution.py:134
  301.7 10.5 %reshape.688 = bf16[32,1,32768]{2,1,0:T(2,128)(2,1)} reshape(bf16[32,2,16384]{2,1,0:T(2,128)(2,1)} %all-to-all-done.6) | data formatting | bytes 4194304
  313.4 171.4 %all-to-all-done.3 = f32[32,1,32768]{2,1,0:T(1,128)} async-done(((f32[32,1,32768]{2,1,0:T(1,128)}), f32[32,1,32768]{2,1,0:T(1,128)}, u32[]{:S(2)}, u32[]{:S(2)}) %all-to-all-start.3) | async-done | bytes 4194336 | tf_op jit(solution)/shard_map/all_to_all | solution.py:134
  484.7 6.6 copy.249
  491.3 6.0 dot_general.86
  497.4 6.8 fusion.20
  504.1 1.1 multiply_reduce_fusion
  505.9 0.7 copy.177
  506.6 10.9 %all-to-all-start.5 = ((f32[32,1,512]{2,1,0:T(1,128)}), f32[32,1,512]{2,1,0:T(1,128)S(1)}, u32[]{:S(2)}, u32[]{:S(2)}) async-start(f32[32,1,512]{2,1,0:T(1,128)} %copy.177), calls=%async_computation.5 | async-start | bytes 131072 | tf_op jit(solution)/shard_map/all_to_all | solution.py:159
  517.5 4.5 convolution_convert_fusion.2
  522.0 8.5 %all-to-all-done.5 = f32[32,1,512]{2,1,0:T(1,128)S(1)} async-done(((f32[32,1,512]{2,1,0:T(1,128)}), f32[32,1,512]{2,1,0:T(1,128)S(1)}, u32[]{:S(2)}, u32[]{:S(2)}) %all-to-all-start.5) | async-done | bytes 65568 | tf_op jit(solution)/shard_map/all_to_all | solution.py:159
  531.1 0.8 fusion.81
  531.9 0.8 copy-done.3
  532.7 2.0 fusion.12
  535.5 1.5 reshape.668
  537.0 3.1 convolution_bitcast_fusion
  540.1 6.3 copy.187
  546.4 6.1 all-to-all-start.7
  552.9 3.7 collective-permute-start.1
  556.7 169.2 %collective-permute-done.1 = bf16[64,512]{1,0:T(8,128)(2,1)S(1)} collective-permute-done((bf16[64,512]{1,0:T(8,128)(2,1)S(1)}, bf16[64,512]{1,0:T(8,128)(2,1)S(1)}, u32[]{:S(2)}, u32[]{:S(2)}) %collective-permute-start.1) | collective-permute-done | bytes 65568 | tf_op jit(solution)/shard_map/ppermute | solution.py:13
  726.5 9.1 %psum.21 = f32[4,191]{1,0:T(4,128)S(1)} all-reduce(f32[4,191]{1,0:T(4,128)S(1)} %reduce_sum.88), channel_id=1, replica_groups=mesh['grp'=4,'seq'=32,'mp'=4] {'grp'}, use_global_device_ids=true, to_apply=%region_10.11 | all-reduce | flops 764 | bytes 6112 | tf_op jit(solution)/shard_map/psum | solution.py:202
  735.6 56.8 %psum.22 = f32[4,191]{1,0:T(4,128)S(1)} all-reduce(f32[4,191]{1,0:T(4,128)S(1)} %psum.21), channel_id=1, replica_groups=mesh['grp'=4,'seq'=32,'mp'=4] {'seq'}, use_global_device_ids=true, to_apply=%region_11.12 | all-reduce | flops 764 | bytes 6112 | tf_op jit(solution)/shard_map/psum | solution.py:203
  793.7 9.1 %psum.23 = f32[]{:T(128)} all-reduce(f32[]{:T(128)} %multiply_reduce_fusion.1), channel_id=1, replica_groups=mesh['grp'=4,'seq'=32,'mp'=4] {'mp'}, use_global_device_ids=true, to_apply=%region_13.14 | all-reduce | flops 1 | bytes 8 | tf_op jit(solution)/shard_map/psum | solution.py:204
  802.8 1.8 convolution_convert_fusion.4
  804.6 4.6 copy.191
  809.2 1.8 multiply_convert_fusion
  811.0 3.8 copy.190
  815.5 6.7 pad_maximum_fusion
  822.2 6.0 fusion.2
  828.2 1.0 fusion.76
  829.6 2.2 collective-permute-start.2
  832.6 1.2 collective-permute-done.2
  (100 shorter events, 15.9 us)
Async XLA Ops:
  4.3 28.5 %all-to-all-start = ((s32[32,1,1]{2,1,0:T(1,128)}), s32[32,1,1]{2,1,0:T(1,128)S(1)}, u32[]{:S(2)}, u32[]{:S(2)}) async-start(s32[32,1,1]{2,1,0:T(1,128)} %copy.156), calls=%async_computation | async-start | bytes 32768 | tf_op jit(solution)/shard_map/all_to_all | solution.py:92
  22.7 11.4 %collective-permute-start = (bf16[2,64,512]{2,1,0:T(8,128)(2,1)S(1)}, bf16[2,64,512]{2,1,0:T(8,128)(2,1)S(1)}, u32[]{:S(2)}, u32[]{:S(2)}) collective-permute-start(bf16[2,64,512]{2,1,0:T(8,128)(2,1)S(1)} %pad_maximum_fusion.3), channel_id=1, source_target_pairs={{4,0},{8,4},{12,8},{16,12},{20,16},{24,20},{28,24},{32,28},{36,32}... | collective-permute-start | bytes 393224 | tf_op jit(solution)/shard_map/ppermute | solution.py:13
  39.3 11.7 %copy-start.5 = (bf16[1,128,512]{2,1,0:T(8,128)(2,1)S(1)}, bf16[1,128,512]{2,1,0:T(8,128)(2,1)}, u32[]{:S(2)}) copy-start(bf16[1,128,512]{2,1,0:T(8,128)(2,1)} %param.6) | copy-start | bytes 393220
  43.8 105.5 %all-to-all-start.1 = ((bf16[32,2,16384]{2,1,0:T(2,128)(2,1)}), bf16[32,2,16384]{2,1,0:T(2,128)(2,1)S(1)}, u32[]{:S(2)}, u32[]{:S(2)}) async-start(bf16[32,2,16384]{2,1,0:T(2,128)(2,1)} %reshape.685), calls=%async_computation.1 | async-start | bytes 4194304 | tf_op jit(solution)/shard_map/all_to_all | solution.py:105
  62.3 98.4 %copy-start.7 = (f32[4,191]{1,0:T(4,128)S(1)}, f32[4,191]{1,0:T(4,128)}, u32[]{:S(2)}) copy-start(f32[4,191]{1,0:T(4,128)} %param.9) | copy-start | bytes 9172
  149.3 11.4 %copy-start = (bf16[32,2,16384]{2,1,0:T(2,128)(2,1)}, bf16[32,2,16384]{2,1,0:T(2,128)(2,1)S(1)}, u32[]{:S(2)}) copy-start(bf16[32,2,16384]{2,1,0:T(2,128)(2,1)S(1)} %all-to-all-done.1) | copy-start | bytes 6291460
  149.3 104.5 %all-to-all-start.6 = ((bf16[32,2,16384]{2,1,0:T(2,128)(2,1)}), bf16[32,2,16384]{2,1,0:T(2,128)(2,1)}, u32[]{:S(2)}, u32[]{:S(2)}) async-start(bf16[32,2,16384]{2,1,0:T(2,128)(2,1)} %reshape.687), calls=%async_computation.6 | async-start | bytes 4194304 | tf_op jit(solution)/shard_map/all_to_all | solution.py:106
  179.1 0.8 copy-start.4
  253.8 18.5 %all-to-all-start.2 = ((f32[32,1,256]{2,1,0:T(1,128)}), f32[32,1,256]{2,1,0:T(1,128)S(1)}, u32[]{:S(2)}, u32[]{:S(2)}) async-start(f32[32,1,256]{2,1,0:T(1,128)} %copy.162), calls=%async_computation.2 | async-start | bytes 65536 | tf_op jit(solution)/shard_map/all_to_all | solution.py:135
  272.3 19.4 %all-to-all-start.4 = ((f32[32,1,256]{2,1,0:T(1,128)}), f32[32,1,256]{2,1,0:T(1,128)S(1)}, u32[]{:S(2)}, u32[]{:S(2)}) async-start(f32[32,1,256]{2,1,0:T(1,128)} %copy.171), calls=%async_computation.4 | async-start | bytes 65536 | tf_op jit(solution)/shard_map/all_to_all | solution.py:136
  291.7 193.0 %all-to-all-start.3 = ((f32[32,1,32768]{2,1,0:T(1,128)}), f32[32,1,32768]{2,1,0:T(1,128)}, u32[]{:S(2)}, u32[]{:S(2)}) async-start(f32[32,1,32768]{2,1,0:T(1,128)} %copy.168), calls=%async_computation.3 | async-start | bytes 8388608 | tf_op jit(solution)/shard_map/all_to_all | solution.py:134
  506.6 23.9 %all-to-all-start.5 = ((f32[32,1,512]{2,1,0:T(1,128)}), f32[32,1,512]{2,1,0:T(1,128)S(1)}, u32[]{:S(2)}, u32[]{:S(2)}) async-start(f32[32,1,512]{2,1,0:T(1,128)} %copy.177), calls=%async_computation.5 | async-start | bytes 131072 | tf_op jit(solution)/shard_map/all_to_all | solution.py:159
  522.0 13.5 %copy-start.1 = (bf16[8,32768]{1,0:T(8,128)(2,1)}, bf16[8,32768]{1,0:T(8,128)(2,1)S(1)}, u32[]{:S(2)}) copy-start(bf16[8,32768]{1,0:T(8,128)(2,1)S(1)} %convolution_convert_fusion.2) | copy-start | bytes 1572868
  531.9 0.8 copy-start.3
  546.4 6.4 copy-start.6
  546.4 256.4 %copy-start.2 = (bf16[8,32768]{1,0:T(8,128)(2,1)S(1)}, bf16[8,32768]{1,0:T(8,128)(2,1)}, u32[]{:S(2)}) copy-start(bf16[8,32768]{1,0:T(8,128)(2,1)} %copy-done.1) | copy-start | bytes 1572868
  546.4 275.8 %all-to-all-start.7 = ((f32[32,1,32768]{2,1,0:T(1,128)}), f32[32,1,32768]{2,1,0:T(1,128)}, u32[]{:S(2)}, u32[]{:S(2)}) async-start(f32[32,1,32768]{2,1,0:T(1,128)} %copy.187), calls=%async_computation.7 | async-start | bytes 8388608 | tf_op jit(solution)/shard_map/all_to_all | solution.py:193
  552.9 173.0 %collective-permute-start.1 = (bf16[64,512]{1,0:T(8,128)(2,1)S(1)}, bf16[64,512]{1,0:T(8,128)(2,1)S(1)}, u32[]{:S(2)}, u32[]{:S(2)}) collective-permute-start(bf16[64,512]{1,0:T(8,128)(2,1)S(1)} %bitcast.224), channel_id=1, source_target_pairs={{0,4},{4,8},{8,12},{12,16},{16,20},{20,24},{24,28},{28,32},{32,36}... | collective-permute-start | bytes 196616 | tf_op jit(solution)/shard_map/ppermute | solution.py:13
  829.6 4.2 collective-permute-start.2
